TPU v7x, 128 devices: a whole 4x4x4 slice. The times are simulated.
128 devices in a mesh: segment: 4 (over x), fsdp: 16 (over y, z_hi, core), rep: 2 (over z_lo).
Axes of the slice: x: 4, y: 4, z: 4 (z_hi: 2, z_lo: 2; z = z_hi * 2 + z_lo), core: 2. Of those that a mesh axis runs over, the one named last changes fastest.
Arguments:
- token_ids: int32 [128, 128], P('fsdp'), may hold values from 0 to 127
- seq_lengths: int32 [128], P('fsdp'), may hold values from 32 to 128, as said below
- quant_scores: int32 [128], P('fsdp'), may hold values from 0 to 64
- embed_table: bfloat16 [128, 4096], replicated, may hold values from -6 to 6
- prior_weight: bfloat16 [4, 4096, 4096], P('segment', None, 'rep'), may hold values from -0.09375 to 0.09375
- prior_gain: float32 [4, 4096], P('segment'), may hold values from 0.25 to 1.75
- final_gain: float32 [4096], replicated, may hold values from 0.25 to 1.75
- head_weight: bfloat16 [4096, 128], replicated, may hold values from -0.25 to 0.25
- agent_down: bfloat16 [4096, 256], P('fsdp'), may hold values from -0.09375 to 0.09375
- agent_up: bfloat16 [4096, 256], P('fsdp'), may hold values from -0.375 to 0.375
Outputs:
- down_gradient: float32 [4096, 256], P(('segment', 'fsdp', 'rep'))
- up_gradient: float32 [4096, 256], P(('segment', 'fsdp', 'rep'))
Inputs may be any that keep to these rules, and one draw needn't show every extreme that they name: `seq_lengths`: every sequence keeps at least 32 tokens, and some sequence in every draw has all 128.
All inputs are finite; a program needn't handle non-finite values.
Results may differ from a plain program's by a relative error of at most 0.0081.
Values may be sent and summed in bfloat16 or wider, within the bound.
No kernel may reach another device: no remote copies, remote signals or barrier semaphores. Data moves between devices by JAX's collectives and lax.ppermute only.
A program may use at most 128 MiB of HBM per device.

v0:
```python
import jax
import jax.numpy as jnp
from jax import lax
from jax.sharding import PartitionSpec as P

LEVELS = 64
epsilon = 1e-05
sigma_weight = 2.0


def passed_along(x, axis, by):
    size = lax.axis_size(axis)
    pairs = [(i, i + by) for i in range(size) if 0 <= i + by < size]
    return lax.ppermute(x, axis, pairs)


def spread(x, axis, root):
    mine = lax.axis_index(axis) == root
    return lax.psum(jnp.where(mine, x, jnp.zeros_like(x)), axis)


def rms_scale(values):
    squares = jnp.mean(values * values, axis=-1, keepdims=True)
    return lax.rsqrt(squares + epsilon)


def lookup_rows(row_ids, embed_table):
    vocab_size = embed_table.shape[0]
    column = jnp.arange(vocab_size, dtype=jnp.int32)
    onehot = (row_ids[:, None] == column[None, :]).astype(jnp.bfloat16)
    return jnp.dot(onehot, embed_table, preferred_element_type=jnp.float32).astype(jnp.bfloat16)


def picked_logprob(logprob, targets):
    vocab_size = logprob.shape[-1]
    column = jnp.arange(vocab_size, dtype=jnp.int32)
    return jnp.sum(jnp.where(column[None, :] == targets[:, None], logprob, 0.0), axis=-1)


def on_device(
    token_ids,
    seq_lengths,
    quant_scores,
    embed_table,
    prior_weight,
    prior_gain,
    final_gain,
    head_weight,
    agent_down,
    agent_up,
):
    segments = lax.axis_size("segment")
    replicas = lax.axis_size("rep")
    segment_pos = lax.axis_index("segment")
    rep_pos = lax.axis_index("rep")
    group_seqs, seq_len = token_ids.shape
    model_width = embed_table.shape[1]
    vocab_size = embed_table.shape[0]
    half_width = prior_weight.shape[2]
    per_device = group_seqs // (segments * replicas)
    micro_count = 4
    total_rows = group_seqs * seq_len
    block_rows = total_rows // micro_count
    tick_count = micro_count + segments - 1
    flat_ids = token_ids.reshape(-1)
    weight_local = prior_weight[0]
    gain_local = prior_gain[0]
    is_first = segment_pos == 0
    is_last = segment_pos == segments - 1

    def apply_segment(current):
        wide_rows = current.astype(jnp.float32)
        normed = (wide_rows * rms_scale(wide_rows) * gain_local).astype(jnp.bfloat16)
        update = jnp.dot(normed, weight_local, preferred_element_type=jnp.float32)
        own_half = lax.dynamic_slice_in_dim(wide_rows, rep_pos * half_width, half_width, 1)
        return (own_half + update).astype(jnp.bfloat16)

    def skip_segment(current):
        return jnp.zeros((block_rows, half_width), jnp.bfloat16)

    def segment_step(tick_pos, received_full):
        micro_pos = tick_pos - segment_pos
        active = (micro_pos >= 0) & (micro_pos < micro_count)
        fresh_pos = jnp.clip(tick_pos, 0, micro_count - 1)
        embedded = lookup_rows(
            lax.dynamic_slice_in_dim(flat_ids, fresh_pos * block_rows, block_rows, 0), embed_table
        )
        current = jnp.where(is_first, embedded, received_full)
        result = lax.cond(active, apply_segment, skip_segment, current)
        return (active, jnp.clip(micro_pos, 0, micro_count - 1), result)

    def store_block(stored, active, slot_pos, block):
        previous = lax.dynamic_slice_in_dim(stored, slot_pos * block_rows, block_rows, 0)
        chosen = jnp.where(active & is_last, block, previous)
        return lax.dynamic_update_slice_in_dim(stored, chosen, slot_pos * block_rows, 0)

    def tick_whole(tick_pos, state_pair):
        incoming, stored = state_pair
        active, slot_pos, result = segment_step(tick_pos, incoming)
        joined = lax.all_gather(result, "rep", axis=1, tiled=True)
        stored = store_block(stored, active, slot_pos, joined)
        incoming = passed_along(joined, "segment", 1)
        return (incoming, stored)

    initial = (
        jnp.zeros((block_rows, model_width), jnp.bfloat16),
        jnp.zeros((total_rows, model_width), jnp.bfloat16),
    )
    final_rows = lax.fori_loop(0, tick_count, tick_whole, initial)[1]
    positions = jnp.arange(seq_len, dtype=jnp.int32)
    next_ids = jnp.concatenate([token_ids[:, 1:], token_ids[:, :1]], axis=1)
    live_mask = (positions[None, :] < seq_lengths[:, None] - 1).astype(jnp.float32)
    counts = (seq_lengths - 1).astype(jnp.float32)

    def prior_scores(rows_bf):
        wide_rows = rows_bf.astype(jnp.float32)
        prior_final = (wide_rows * rms_scale(wide_rows) * final_gain).astype(jnp.bfloat16)
        logprob = jax.nn.log_softmax(
            jnp.dot(prior_final, head_weight, preferred_element_type=jnp.float32), axis=-1
        )
        token_terms = picked_logprob(logprob, next_ids.reshape(-1)).reshape(group_seqs, seq_len)
        return jnp.sum(token_terms * live_mask, axis=1) / counts

    def no_scores(rows_bf):
        return jnp.zeros((group_seqs,), jnp.float32)

    prior_group = lax.cond(is_last, prior_scores, no_scores, final_rows)
    prior_group = spread(prior_group, "segment", segments - 1)
    own_seq = (segment_pos * replicas + rep_pos) * per_device
    prior_mine = lax.dynamic_slice_in_dim(prior_group, own_seq, per_device, 0)
    mine_ids = lax.dynamic_slice_in_dim(token_ids, own_seq, per_device, 0).reshape(-1)
    mine_next = lax.dynamic_slice_in_dim(next_ids, own_seq, per_device, 0).reshape(-1)
    mine_live = lax.dynamic_slice_in_dim(live_mask, own_seq, per_device, 0)
    mine_counts = lax.dynamic_slice_in_dim(counts, own_seq, per_device, 0)
    mine_scores = lax.dynamic_slice_in_dim(quant_scores, own_seq, per_device, 0)
    down_full, up_full = (
        lax.all_gather(agent_down, "fsdp", axis=0, tiled=True),
        lax.all_gather(agent_up, "fsdp", axis=0, tiled=True),
    )
    start_wide = lookup_rows(mine_ids, embed_table).astype(jnp.float32)
    unit_rows = (start_wide * rms_scale(start_wide)).astype(jnp.bfloat16)
    latent = jnp.dot(unit_rows, down_full, preferred_element_type=jnp.float32).astype(jnp.bfloat16)
    hidden = start_wide + lax.dot_general(
        latent, up_full, (((1,), (1,)), ((), ())), preferred_element_type=jnp.float32
    )
    inverse = rms_scale(hidden)
    agent_final = (hidden * inverse * final_gain).astype(jnp.bfloat16)
    logprob = jax.nn.log_softmax(
        jnp.dot(agent_final, head_weight, preferred_element_type=jnp.float32), axis=-1
    )
    agent_ll = (
        jnp.sum(picked_logprob(logprob, mine_next).reshape(per_device, seq_len) * mine_live, axis=1)
        / mine_counts
    )
    margin = prior_mine + sigma_weight * mine_scores.astype(jnp.float32) / LEVELS - agent_ll
    row_factor = ((2.0 * margin / mine_counts)[:, None] * mine_live).reshape(-1)
    column = jnp.arange(vocab_size, dtype=jnp.int32)
    onehot_next = (mine_next[:, None] == column[None, :]).astype(jnp.float32)
    logit_grad = (row_factor[:, None] * (jnp.exp(logprob) - onehot_next)).astype(jnp.bfloat16)
    scaled_grad = (
        lax.dot_general(
            logit_grad, head_weight, (((1,), (1,)), ((), ())), preferred_element_type=jnp.float32
        )
        * final_gain
    )
    hidden_grad = (
        inverse * scaled_grad
        - hidden
        * inverse
        * inverse
        * inverse
        * jnp.mean(hidden * scaled_grad, axis=-1, keepdims=True)
    ).astype(jnp.bfloat16)
    up_grad = lax.dot_general(
        hidden_grad, latent, (((0,), (0,)), ((), ())), preferred_element_type=jnp.float32
    )
    latent_grad = jnp.dot(hidden_grad, up_full, preferred_element_type=jnp.float32).astype(
        jnp.bfloat16
    )
    down_grad = lax.dot_general(
        unit_rows, latent_grad, (((0,), (0,)), ((), ())), preferred_element_type=jnp.float32
    )
    down_share, up_share = (
        lax.psum_scatter(down_grad, ("segment", "fsdp", "rep"), scatter_dimension=0, tiled=True),
        lax.psum_scatter(up_grad, ("segment", "fsdp", "rep"), scatter_dimension=0, tiled=True),
    )
    return (down_share, up_share)


def solution(mesh):
    placed = (
        P("fsdp", None),
        P("fsdp"),
        P("fsdp"),
        P(),
        P("segment", None, "rep"),
        P("segment", None),
        P(),
        P(),
        P("fsdp", None),
        P("fsdp", None),
    )
    return jax.shard_map(
        on_device,
        mesh=mesh,
        in_specs=placed,
        out_specs=(P(("segment", "fsdp", "rep"), None), P(("segment", "fsdp", "rep"), None)),
        check_vma=False,
    )
```

profile of v0, /device:TPU:0, one launch (start us, length us, event | category | flops | bytes accessed | tf_op | source)
XLA Modules:
  0.0 2145.9 jit_solution(12127194747232947936)
XLA Ops:
  8.3 4.3 broadcast_in_dim.30
  12.6 715.6 %while.15 = (s32[]{:T(128)}, bf16[256,4096]{1,0:T(8,128)(2,1)S(1)}, bf16[1024,4096]{1,0:T(8,128)(2,1)}, s32[]{:T(128)}, s32[1024]{0:T(1024)S(1)}, /*index=5*/bf1...) while((s32[]{:T(128)}, bf16[256,4096]{1,0:T(8,128)(2,1)S(1)}, ...), condition=%wide.region_6.7_spmd, body=%wide.region_2.6_spmd.sunk | while | flops 4573921792 | bytes 63987248 | solution.py:109
  13.5 14.8 conditional.4
  16.2 12.1 fusion
  29.3 35.9 %all-gather.8.cloned.1.call-done = bf16[256,4096]{1,0:T(8,128)(2,1)} async-done(((bf16[256,2048]{1,0:T(8,128)(2,1)}), bf16[256,4096]{1,0:T(8,128)(2,1)}) %all-gather.8.cloned.1.call-update) | async-done | bytes 2097168 | tf_op jit(solution)/shard_map/while/body/eval_jaxpr/all_gather | solution.py:100
  68.7 3.8 select_dynamic-update-slice_fusion.2
  72.4 41.1 %collective-permute-done = bf16[256,4096]{1,0:T(8,128)(2,1)S(1)} collective-permute-done((bf16[256,4096]{1,0:T(8,128)(2,1)}, bf16[256,4096]{1,0:T(8,128)(2,1)S(1)}, u32[]{:S(2)}, u32[]{:S(2)}) %collective-permute-start) | collective-permute-done | bytes 2097184 | tf_op jit(solution)/shard_map/while/body/eval_jaxpr/ppermute | solution.py:14
  114.4 14.8 conditional.4
  117.0 12.1 fusion
  130.2 36.2 %all-gather.8.cloned.1.call-done = bf16[256,4096]{1,0:T(8,128)(2,1)} async-done(((bf16[256,2048]{1,0:T(8,128)(2,1)}), bf16[256,4096]{1,0:T(8,128)(2,1)}) %all-gather.8.cloned.1.call-update) | async-done | bytes 2097168 | tf_op jit(solution)/shard_map/while/body/eval_jaxpr/all_gather | solution.py:100
  173.6 41.2 %collective-permute-done = bf16[256,4096]{1,0:T(8,128)(2,1)S(1)} collective-permute-done((bf16[256,4096]{1,0:T(8,128)(2,1)}, bf16[256,4096]{1,0:T(8,128)(2,1)S(1)}, u32[]{:S(2)}, u32[]{:S(2)}) %collective-permute-start) | collective-permute-done | bytes 2097184 | tf_op jit(solution)/shard_map/while/body/eval_jaxpr/ppermute | solution.py:14
  215.6 14.8 conditional.4
  218.3 12.1 fusion
  231.4 37.7 %all-gather.8.cloned.1.call-done = bf16[256,4096]{1,0:T(8,128)(2,1)} async-done(((bf16[256,2048]{1,0:T(8,128)(2,1)}), bf16[256,4096]{1,0:T(8,128)(2,1)}) %all-gather.8.cloned.1.call-update) | async-done | bytes 2097168 | tf_op jit(solution)/shard_map/while/body/eval_jaxpr/all_gather | solution.py:100
  276.4 41.1 %collective-permute-done = bf16[256,4096]{1,0:T(8,128)(2,1)S(1)} collective-permute-done((bf16[256,4096]{1,0:T(8,128)(2,1)}, bf16[256,4096]{1,0:T(8,128)(2,1)S(1)}, u32[]{:S(2)}, u32[]{:S(2)}) %collective-permute-start) | collective-permute-done | bytes 2097184 | tf_op jit(solution)/shard_map/while/body/eval_jaxpr/ppermute | solution.py:14
  318.3 14.8 conditional.4
  321.0 12.1 fusion
  334.1 37.7 %all-gather.8.cloned.1.call-done = bf16[256,4096]{1,0:T(8,128)(2,1)} async-done(((bf16[256,2048]{1,0:T(8,128)(2,1)}), bf16[256,4096]{1,0:T(8,128)(2,1)}) %all-gather.8.cloned.1.call-update) | async-done | bytes 2097168 | tf_op jit(solution)/shard_map/while/body/eval_jaxpr/all_gather | solution.py:100
  375.4 3.7 select_dynamic-update-slice_fusion.2
  379.1 41.1 %collective-permute-done = bf16[256,4096]{1,0:T(8,128)(2,1)S(1)} collective-permute-done((bf16[256,4096]{1,0:T(8,128)(2,1)}, bf16[256,4096]{1,0:T(8,128)(2,1)S(1)}, u32[]{:S(2)}, u32[]{:S(2)}) %collective-permute-start) | collective-permute-done | bytes 2097184 | tf_op jit(solution)/shard_map/while/body/eval_jaxpr/ppermute | solution.py:14
  422.2 52.4 %all-gather.8.cloned.1.call-done = bf16[256,4096]{1,0:T(8,128)(2,1)} async-done(((bf16[256,2048]{1,0:T(8,128)(2,1)}), bf16[256,4096]{1,0:T(8,128)(2,1)}) %all-gather.8.cloned.1.call-update) | async-done | bytes 2097168 | tf_op jit(solution)/shard_map/while/body/eval_jaxpr/all_gather | solution.py:100
  481.8 41.1 %collective-permute-done = bf16[256,4096]{1,0:T(8,128)(2,1)S(1)} collective-permute-done((bf16[256,4096]{1,0:T(8,128)(2,1)}, bf16[256,4096]{1,0:T(8,128)(2,1)S(1)}, u32[]{:S(2)}, u32[]{:S(2)}) %collective-permute-start) | collective-permute-done | bytes 2097184 | tf_op jit(solution)/shard_map/while/body/eval_jaxpr/ppermute | solution.py:14
  524.9 52.4 %all-gather.8.cloned.1.call-done = bf16[256,4096]{1,0:T(8,128)(2,1)} async-done(((bf16[256,2048]{1,0:T(8,128)(2,1)}), bf16[256,4096]{1,0:T(8,128)(2,1)}) %all-gather.8.cloned.1.call-update) | async-done | bytes 2097168 | tf_op jit(solution)/shard_map/while/body/eval_jaxpr/all_gather | solution.py:100
  584.6 41.1 %collective-permute-done = bf16[256,4096]{1,0:T(8,128)(2,1)S(1)} collective-permute-done((bf16[256,4096]{1,0:T(8,128)(2,1)}, bf16[256,4096]{1,0:T(8,128)(2,1)S(1)}, u32[]{:S(2)}, u32[]{:S(2)}) %collective-permute-start) | collective-permute-done | bytes 2097184 | tf_op jit(solution)/shard_map/while/body/eval_jaxpr/ppermute | solution.py:14
  627.7 52.1 %all-gather.8.cloned.1.call-done = bf16[256,4096]{1,0:T(8,128)(2,1)} async-done(((bf16[256,2048]{1,0:T(8,128)(2,1)}), bf16[256,4096]{1,0:T(8,128)(2,1)}) %all-gather.8.cloned.1.call-update) | async-done | bytes 2097168 | tf_op jit(solution)/shard_map/while/body/eval_jaxpr/all_gather | solution.py:100
  687.0 41.1 %collective-permute-done = bf16[256,4096]{1,0:T(8,128)(2,1)S(1)} collective-permute-done((bf16[256,4096]{1,0:T(8,128)(2,1)}, bf16[256,4096]{1,0:T(8,128)(2,1)S(1)}, u32[]{:S(2)}, u32[]{:S(2)}) %collective-permute-start) | collective-permute-done | bytes 2097184 | tf_op jit(solution)/shard_map/while/body/eval_jaxpr/ppermute | solution.py:14
  729.6 21.7 %psum.7 = f32[8]{0:T(128)S(1)} all-reduce(f32[8]{0:T(128)S(1)} %broadcast_select_fusion), channel_id=1, replica_groups=mesh['segment'=4,'fsdp'=16,'rep'=2] {'segment'}, use_global_device_ids=true, to_apply=%region_14.15 | all-reduce | flops 8 | bytes 64 | tf_op jit(solution)/shard_map/psum | solution.py:19
  755.1 26.0 %all-gather.4.cloned.1.call-done = bf16[4096,256]{1,0:T(8,128)(2,1)} async-done(((bf16[256,256]{1,0:T(8,128)(2,1)}), bf16[4096,256]{1,0:T(8,128)(2,1)}) %all-gather.4.cloned.1.call-update) | async-done | bytes 2097168 | tf_op jit(solution)/shard_map/all_gather | solution.py:137
  783.2 47.1 %all-gather.6.cloned.1.call-done = bf16[4096,256]{1,0:T(8,128)(2,1)} async-done(((bf16[256,256]{1,0:T(8,128)(2,1)}), bf16[4096,256]{1,0:T(8,128)(2,1)}) %all-gather.6.cloned.1.call-update) | async-done | bytes 2097168 | tf_op jit(solution)/shard_map/all_gather | solution.py:138
  837.4 5.2 fusion.13
  845.4 646.0 %reduce-scatter.3.cloned.1.call-done = f32[32,256]{1,0:T(8,128)} async-done(((f32[4096,256]{1,0:T(8,128)}), f32[32,256]{1,0:T(8,128)}) %reduce-scatter.3.cloned.1.call-update) | async-done | bytes 32784 | tf_op jit(solution)/shard_map/reduce_scatter | solution.py:184
  1491.3 647.0 %reduce-scatter.5.cloned.1.call-done = f32[32,256]{1,0:T(8,128)} async-done(((f32[4096,256]{1,0:T(8,128)}), f32[32,256]{1,0:T(8,128)}) %reduce-scatter.5.cloned.1.call-update) | async-done | bytes 32784 | tf_op jit(solution)/shard_map/reduce_scatter | solution.py:185
  (117 shorter events, 81.1 us)
Async XLA Ops:
  8.2 4.3 copy-start.2
  8.3 4.3 copy-start.5
  8.3 4.3 copy-start.6
  12.6 716.9 %copy-start.7 = (s32[8]{0:T(128)S(1)}, s32[8]{0:T(128)}, u32[]{:S(2)}) copy-start(s32[8]{0:T(128)} %param.17) | copy-start | bytes 100
  12.6 717.0 %copy-start.4 = (f32[4096]{0:T(1024)S(1)}, f32[4096]{0:T(1024)}, u32[]{:S(2)}) copy-start(f32[4096]{0:T(1024)} %param.22) | copy-start | bytes 49156
  12.6 52.6 %all-gather.8.cloned.1.call-start = ((), (), s32[]{:S(2)}) async-start(), calls=%async_computation.6 | async-start | bytes 3145728 | tf_op jit(solution)/shard_map/while/body/eval_jaxpr/all_gather | solution.py:100
  28.3 1.0 copy-start
  65.2 48.4 %collective-permute-start = (bf16[256,4096]{1,0:T(8,128)(2,1)}, bf16[256,4096]{1,0:T(8,128)(2,1)S(1)}, u32[]{:S(2)}, u32[]{:S(2)}) collective-permute-start(bf16[256,4096]{1,0:T(8,128)(2,1)} %all-gather.8.cloned.1.call-done), channel_id=1, source_target_pairs={{0,32},{32,64},{64,96},{1,33},{33,65},{65,97},{2,34},{34,66},{66,9... | collective-permute-start | bytes 6291464 | tf_op jit(solution)/shard_map/while/body/eval_jaxpr/ppermute | solution.py:14
  113.5 52.8 %all-gather.8.cloned.1.call-start = ((), (), s32[]{:S(2)}) async-start(), calls=%async_computation.6 | async-start | bytes 3145728 | tf_op jit(solution)/shard_map/while/body/eval_jaxpr/all_gather | solution.py:100
  129.2 1.0 copy-start
  166.4 48.4 %collective-permute-start = (bf16[256,4096]{1,0:T(8,128)(2,1)}, bf16[256,4096]{1,0:T(8,128)(2,1)S(1)}, u32[]{:S(2)}, u32[]{:S(2)}) collective-permute-start(bf16[256,4096]{1,0:T(8,128)(2,1)} %all-gather.8.cloned.1.call-done), channel_id=1, source_target_pairs={{0,32},{32,64},{64,96},{1,33},{33,65},{65,97},{2,34},{34,66},{66,9... | collective-permute-start | bytes 6291464 | tf_op jit(solution)/shard_map/while/body/eval_jaxpr/ppermute | solution.py:14
  214.8 54.3 %all-gather.8.cloned.1.call-start = ((), (), s32[]{:S(2)}) async-start(), calls=%async_computation.6 | async-start | bytes 3145728 | tf_op jit(solution)/shard_map/while/body/eval_jaxpr/all_gather | solution.py:100
  230.4 1.0 copy-start
  269.1 48.4 %collective-permute-start = (bf16[256,4096]{1,0:T(8,128)(2,1)}, bf16[256,4096]{1,0:T(8,128)(2,1)S(1)}, u32[]{:S(2)}, u32[]{:S(2)}) collective-permute-start(bf16[256,4096]{1,0:T(8,128)(2,1)} %all-gather.8.cloned.1.call-done), channel_id=1, source_target_pairs={{0,32},{32,64},{64,96},{1,33},{33,65},{65,97},{2,34},{34,66},{66,9... | collective-permute-start | bytes 6291464 | tf_op jit(solution)/shard_map/while/body/eval_jaxpr/ppermute | solution.py:14
  317.5 54.3 %all-gather.8.cloned.1.call-start = ((), (), s32[]{:S(2)}) async-start(), calls=%async_computation.6 | async-start | bytes 3145728 | tf_op jit(solution)/shard_map/while/body/eval_jaxpr/all_gather | solution.py:100
  333.1 1.0 copy-start
  371.8 48.4 %collective-permute-start = (bf16[256,4096]{1,0:T(8,128)(2,1)}, bf16[256,4096]{1,0:T(8,128)(2,1)S(1)}, u32[]{:S(2)}, u32[]{:S(2)}) collective-permute-start(bf16[256,4096]{1,0:T(8,128)(2,1)} %all-gather.8.cloned.1.call-done), channel_id=1, source_target_pairs={{0,32},{32,64},{64,96},{1,33},{33,65},{65,97},{2,34},{34,66},{66,9... | collective-permute-start | bytes 6291464 | tf_op jit(solution)/shard_map/while/body/eval_jaxpr/ppermute | solution.py:14
  420.2 54.3 %all-gather.8.cloned.1.call-start = ((), (), s32[]{:S(2)}) async-start(), calls=%async_computation.6 | async-start | bytes 3145728 | tf_op jit(solution)/shard_map/while/body/eval_jaxpr/all_gather | solution.py:100
  421.2 1.0 copy-start
  474.6 48.4 %collective-permute-start = (bf16[256,4096]{1,0:T(8,128)(2,1)}, bf16[256,4096]{1,0:T(8,128)(2,1)S(1)}, u32[]{:S(2)}, u32[]{:S(2)}) collective-permute-start(bf16[256,4096]{1,0:T(8,128)(2,1)} %all-gather.8.cloned.1.call-done), channel_id=1, source_target_pairs={{0,32},{32,64},{64,96},{1,33},{33,65},{65,97},{2,34},{34,66},{66,9... | collective-permute-start | bytes 6291464 | tf_op jit(solution)/shard_map/while/body/eval_jaxpr/ppermute | solution.py:14
  523.0 54.3 %all-gather.8.cloned.1.call-start = ((), (), s32[]{:S(2)}) async-start(), calls=%async_computation.6 | async-start | bytes 3145728 | tf_op jit(solution)/shard_map/while/body/eval_jaxpr/all_gather | solution.py:100
  523.9 1.0 copy-start
  577.3 48.4 %collective-permute-start = (bf16[256,4096]{1,0:T(8,128)(2,1)}, bf16[256,4096]{1,0:T(8,128)(2,1)S(1)}, u32[]{:S(2)}, u32[]{:S(2)}) collective-permute-start(bf16[256,4096]{1,0:T(8,128)(2,1)} %all-gather.8.cloned.1.call-done), channel_id=1, source_target_pairs={{0,32},{32,64},{64,96},{1,33},{33,65},{65,97},{2,34},{34,66},{66,9... | collective-permute-start | bytes 6291464 | tf_op jit(solution)/shard_map/while/body/eval_jaxpr/ppermute | solution.py:14
  625.7 54.1 %all-gather.8.cloned.1.call-start = ((), (), s32[]{:S(2)}) async-start(), calls=%async_computation.6 | async-start | bytes 3145728 | tf_op jit(solution)/shard_map/while/body/eval_jaxpr/all_gather | solution.py:100
  626.7 1.0 copy-start
  679.7 48.4 %collective-permute-start = (bf16[256,4096]{1,0:T(8,128)(2,1)}, bf16[256,4096]{1,0:T(8,128)(2,1)S(1)}, u32[]{:S(2)}, u32[]{:S(2)}) collective-permute-start(bf16[256,4096]{1,0:T(8,128)(2,1)} %all-gather.8.cloned.1.call-done), channel_id=1, source_target_pairs={{0,32},{32,64},{64,96},{1,33},{33,65},{65,97},{2,34},{34,66},{66,9... | collective-permute-start | bytes 6291464 | tf_op jit(solution)/shard_map/while/body/eval_jaxpr/ppermute | solution.py:14
  728.1 52.9 %all-gather.4.cloned.1.call-start = ((), (), s32[]{:S(2)}) async-start(), calls=%async_computation.2 | async-start | bytes 2228224 | tf_op jit(solution)/shard_map/all_gather | solution.py:137
  728.7 101.5 %all-gather.6.cloned.1.call-start = ((), (), s32[]{:S(2)}) async-start(), calls=%async_computation.3 | async-start | bytes 2228224 | tf_op jit(solution)/shard_map/all_gather | solution.py:138
  729.3 762.0 %reduce-scatter.3.cloned.1.call-start = ((), (), s32[]{:S(2)}) async-start(), calls=%async_computation.4 | async-start | bytes 4227072 | tf_op jit(solution)/shard_map/reduce_scatter | solution.py:184
  729.6 23.0 %copy-start.8 = (s32[8]{0:T(128)S(1)}, s32[8]{0:T(128)}, u32[]{:S(2)}) copy-start(s32[8]{0:T(128)} %param.18) | copy-start | bytes 100
  783.1 49.6 %copy-start.3 = (bf16[4096,128]{1,0:T(8,128)(2,1)S(1)}, bf16[4096,128]{1,0:T(8,128)(2,1)}, u32[]{:S(2)}) copy-start(bf16[4096,128]{1,0:T(8,128)(2,1)} %param.23) | copy-start | bytes 3145732
  842.6 1295.7 %reduce-scatter.5.cloned.1.call-start = ((), (), s32[]{:S(2)}) async-start(), calls=%async_computation.5 | async-start | bytes 4227072 | tf_op jit(solution)/shard_map/reduce_scatter | solution.py:185
Sparse Core Ops, SparseCore 0:
  29.4 35.7 all-gather.7
  130.3 36.0 all-gather.7
  231.5 37.5 all-gather.7
  334.2 37.5 all-gather.7
  422.4 52.1 all-gather.7
  525.1 52.1 all-gather.7
  628.1 51.5 all-gather.7
Sparse Core Ops, SparseCore 1:
  731.0 50.0 all-gather.3
  783.3 46.8 all-gather.5
  842.7 648.6 reduce-scatter.2
  1494.3 644.0 reduce-scatter.4
where the time goes:
time: 2150 us
  waiting for transfers between devices  1960 us (91%)
  matrix products  67.8 us (3%)
  other arithmetic  38.2 us (2%)
  starting transfers between devices  24.6 us (1%)
  blocking collectives  21.7 us (1%)
    reduce_scatter x1, waiting for transfers between devices, on_device(): lax.psum_scatter(up_grad, ('segment', 'fsdp', 'rep'), scatter_dimension=0...  647 us
    reduce_scatter x1, waiting for transfers between devices, on_device(): lax.psum_scatter(down_grad, ('segment', 'fsdp', 'rep'), scatter_dimension...  646 us
    all_gather x7, waiting for transfers between devices, tick_whole(): joined = lax.all_gather(result, 'rep', axis=1, tiled=True)  304 us
    ppermute x7, waiting for transfers between devices, passed_along(): return lax.ppermute(x, axis, pairs)  288 us
    dot_general x4, matrix products, apply_segment(): update = jnp.dot(normed, weight_local, preferred_element_type=jnp.float32)  48.4 us
    all_gather x1, waiting for transfers between devices, on_device(): lax.all_gather(agent_up, 'fsdp', axis=0, tiled=True)  47.1 us
  transfers between devices with their start and end apart: 18, of which 18 were waited for; matrix products, arithmetic and copies ran while one was open for 2% of the time, Pallas kernels for 0%

commit v1 on v0

--- a/solution.py
+++ b/solution.py
@@ -97,7 +97,9 @@
     def tick_whole(tick_pos, state_pair):
         incoming, stored = state_pair
         active, slot_pos, result = segment_step(tick_pos, incoming)
-        joined = lax.all_gather(result, "rep", axis=1, tiled=True)
+        joined = jnp.concatenate(
+            lax.all_to_all(jnp.stack([result] * lax.axis_size("rep")), "rep", 0, 0), axis=1
+        )
         stored = store_block(stored, active, slot_pos, joined)
         incoming = passed_along(joined, "segment", 1)
         return (incoming, stored)

time: 2150 us -> 1960 us (0.912)
  waiting for transfers between devices: 1960 us -> 1540 us
  blocking collectives: 21.7 us -> 205 us
  starting transfers between devices: 24.6 us -> 75.4 us
    all_gather x7 -> x0, waiting for transfers between devices: 304 us -> none  [tick_whole(): joined = lax.all_gather(result, 'rep', axis=1, tiled=True)]
    all_to_all x0 -> x7, blocking collectives: none -> 165 us  [tick_whole(): lax.all_to_all(jnp.stack([result] * lax.axis_size('rep')), 'rep', 0, 0)]
    ppermute x7, starting transfers between devices: 24.5 us -> 75.2 us  [passed_along(): return lax.ppermute(x, axis, pairs)]
    ppermute x7, waiting for transfers between devices: 288 us -> 238 us  [passed_along(): return lax.ppermute(x, axis, pairs)]
    all_gather x1, waiting for transfers between devices: 47.1 us -> 0.02 us  [on_device(): lax.all_gather(agent_up, 'fsdp', axis=0, tiled=True)]
    all_gather x1, waiting for transfers between devices: 26 us -> 0.02 us  [on_device(): lax.all_gather(agent_down, 'fsdp', axis=0, tiled=True)]
  transfers between devices with their start and end apart: 18 -> 11, of which waited for: 18 -> 9; matrix products, arithmetic and copies ran while one was open for 2% -> 6% of each run, Pallas kernels for 0% -> 0%
where the time goes in v1:
time: 1960 us
  waiting for transfers between devices  1540 us (79%)
  blocking collectives  205 us (10%)
  starting transfers between devices  75.4 us (4%)
  matrix products  68.1 us (3%)
  other arithmetic  40.8 us (2%)
    reduce_scatter x1, waiting for transfers between devices, on_device(): lax.psum_scatter(down_grad, ('segment', 'fsdp', 'rep'), scatter_dimension...  650 us
    reduce_scatter x1, waiting for transfers between devices, on_device(): lax.psum_scatter(up_grad, ('segment', 'fsdp', 'rep'), scatter_dimension=0...  649 us
    ppermute x7, waiting for transfers between devices, passed_along(): return lax.ppermute(x, axis, pairs)  238 us
    all_to_all x7, blocking collectives, tick_whole(): lax.all_to_all(jnp.stack([result] * lax.axis_size('rep')), 'rep', 0, 0)  165 us
    ppermute x7, starting transfers between devices, passed_along(): return lax.ppermute(x, axis, pairs)  75.2 us
    dot_general x4, matrix products, apply_segment(): update = jnp.dot(normed, weight_local, preferred_element_type=jnp.float32)  48.6 us
    psum x1, blocking collectives, spread(): return lax.psum(jnp.where(mine, x, jnp.zeros_like(x)), axis)  40.7 us
  transfers between devices with their start and end apart: 11, of which 9 were waited for; matrix products, arithmetic and copies ran while one was open for 6% of the time, Pallas kernels for 0%

profile of v1, /device:TPU:0, one launch (start us, length us, event | category | flops | bytes accessed | tf_op | source)
XLA Modules:
  0.0 1960.5 jit_solution(17106412016440416015)
XLA Ops:
  16.8 576.4 %while.15 = (s32[]{:T(128)}, bf16[256,4096]{1,0:T(8,128)(2,1)}, bf16[1024,4096]{1,0:T(8,128)(2,1)}, s32[]{:T(128)}, s32[1024]{0:T(1024)}, /*index=5*/bf16[128,40...) while((s32[]{:T(128)}, bf16[256,4096]{1,0:T(8,128)(2,1)}, ...), condition=%wide.region_6.7_spmd, body=%wide.region_2.6_spmd.sunk | while | flops 4574970368 | bytes 61890028 | solution.py:111
  18.3 15.0 conditional.4
  21.0 12.3 fusion
  33.5 33.6 %all_to_all.10 = bf16[2,256,2048]{2,1,0:T(8,128)(2,1)S(1)} all-to-all(bf16[2,256,2048]{2,1,0:T(8,128)(2,1)S(1)} %pad_maximum_fusion.2), channel_id=1, replica_groups=mesh['segment'=4,'fsdp'=16,'rep'=2] {'rep'}, dimensions={0} | all-to-all | bytes 4194304 | tf_op jit(solution)/shard_map/while/body/eval_jaxpr/all_to_all | solution.py:101
  73.6 39.1 %collective-permute-done = bf16[256,4096]{1,0:T(8,128)(2,1)} collective-permute-done((bf16[256,4096]{1,0:T(8,128)(2,1)S(1)}, bf16[256,4096]{1,0:T(8,128)(2,1)}, u32[]{:S(2)}, u32[]{:S(2)}) %collective-permute-start) | collective-permute-done | bytes 2097184 | tf_op jit(solution)/shard_map/while/body/eval_jaxpr/ppermute | solution.py:14
  114.2 14.8 conditional.4
  116.9 12.1 fusion
  129.2 26.1 %all_to_all.10 = bf16[2,256,2048]{2,1,0:T(8,128)(2,1)S(1)} all-to-all(bf16[2,256,2048]{2,1,0:T(8,128)(2,1)S(1)} %pad_maximum_fusion.2), channel_id=1, replica_groups=mesh['segment'=4,'fsdp'=16,'rep'=2] {'rep'}, dimensions={0} | all-to-all | bytes 4194304 | tf_op jit(solution)/shard_map/while/body/eval_jaxpr/all_to_all | solution.py:101
  155.4 7.4 collective-permute-start
  166.6 37.4 %collective-permute-done = bf16[256,4096]{1,0:T(8,128)(2,1)} collective-permute-done((bf16[256,4096]{1,0:T(8,128)(2,1)S(1)}, bf16[256,4096]{1,0:T(8,128)(2,1)}, u32[]{:S(2)}, u32[]{:S(2)}) %collective-permute-start) | collective-permute-done | bytes 2097184 | tf_op jit(solution)/shard_map/while/body/eval_jaxpr/ppermute | solution.py:14
  205.5 14.8 conditional.4
  208.2 12.1 fusion
  220.5 24.4 %all_to_all.10 = bf16[2,256,2048]{2,1,0:T(8,128)(2,1)S(1)} all-to-all(bf16[2,256,2048]{2,1,0:T(8,128)(2,1)S(1)} %pad_maximum_fusion.2), channel_id=1, replica_groups=mesh['segment'=4,'fsdp'=16,'rep'=2] {'rep'}, dimensions={0} | all-to-all | bytes 4194304 | tf_op jit(solution)/shard_map/while/body/eval_jaxpr/all_to_all | solution.py:101
  245.0 7.4 collective-permute-start
  256.2 35.7 %collective-permute-done = bf16[256,4096]{1,0:T(8,128)(2,1)} collective-permute-done((bf16[256,4096]{1,0:T(8,128)(2,1)S(1)}, bf16[256,4096]{1,0:T(8,128)(2,1)}, u32[]{:S(2)}, u32[]{:S(2)}) %collective-permute-start) | collective-permute-done | bytes 2097184 | tf_op jit(solution)/shard_map/while/body/eval_jaxpr/ppermute | solution.py:14
  293.3 14.8 conditional.4
  296.0 12.1 fusion
  308.3 22.7 %all_to_all.10 = bf16[2,256,2048]{2,1,0:T(8,128)(2,1)S(1)} all-to-all(bf16[2,256,2048]{2,1,0:T(8,128)(2,1)S(1)} %pad_maximum_fusion.2), channel_id=1, replica_groups=mesh['segment'=4,'fsdp'=16,'rep'=2] {'rep'}, dimensions={0} | all-to-all | bytes 4194304 | tf_op jit(solution)/shard_map/while/body/eval_jaxpr/all_to_all | solution.py:101
  331.2 7.4 collective-permute-start
  342.3 33.9 %collective-permute-done = bf16[256,4096]{1,0:T(8,128)(2,1)} collective-permute-done((bf16[256,4096]{1,0:T(8,128)(2,1)S(1)}, bf16[256,4096]{1,0:T(8,128)(2,1)}, u32[]{:S(2)}, u32[]{:S(2)}) %collective-permute-start) | collective-permute-done | bytes 2097184 | tf_op jit(solution)/shard_map/while/body/eval_jaxpr/ppermute | solution.py:14
  378.1 21.0 %all_to_all.10 = bf16[2,256,2048]{2,1,0:T(8,128)(2,1)S(1)} all-to-all(bf16[2,256,2048]{2,1,0:T(8,128)(2,1)S(1)} %pad_maximum_fusion.2), channel_id=1, replica_groups=mesh['segment'=4,'fsdp'=16,'rep'=2] {'rep'}, dimensions={0} | all-to-all | bytes 4194304 | tf_op jit(solution)/shard_map/while/body/eval_jaxpr/all_to_all | solution.py:101
  399.2 22.1 %collective-permute-start = (bf16[256,4096]{1,0:T(8,128)(2,1)S(1)}, bf16[256,4096]{1,0:T(8,128)(2,1)}, u32[]{:S(2)}, u32[]{:S(2)}) collective-permute-start(bf16[256,4096]{1,0:T(8,128)(2,1)S(1)} %bitcast.46), channel_id=1, source_target_pairs={{0,32},{32,64},{64,96},{1,33},{33,65},{65,97},{2,34},{34,66},{66,9... | collective-permute-start | bytes 6291464 | tf_op jit(solution)/shard_map/while/body/eval_jaxpr/ppermute | solution.py:14
  425.0 32.2 %collective-permute-done = bf16[256,4096]{1,0:T(8,128)(2,1)} collective-permute-done((bf16[256,4096]{1,0:T(8,128)(2,1)S(1)}, bf16[256,4096]{1,0:T(8,128)(2,1)}, u32[]{:S(2)}, u32[]{:S(2)}) %collective-permute-start) | collective-permute-done | bytes 2097184 | tf_op jit(solution)/shard_map/while/body/eval_jaxpr/ppermute | solution.py:14
  459.1 19.2 all_to_all.10
  478.5 5.9 collective-permute-start
  488.1 30.5 %collective-permute-done = bf16[256,4096]{1,0:T(8,128)(2,1)} collective-permute-done((bf16[256,4096]{1,0:T(8,128)(2,1)S(1)}, bf16[256,4096]{1,0:T(8,128)(2,1)}, u32[]{:S(2)}, u32[]{:S(2)}) %collective-permute-start) | collective-permute-done | bytes 2097184 | tf_op jit(solution)/shard_map/while/body/eval_jaxpr/ppermute | solution.py:14
  520.5 17.6 all_to_all.10
  538.2 22.3 %collective-permute-start = (bf16[256,4096]{1,0:T(8,128)(2,1)S(1)}, bf16[256,4096]{1,0:T(8,128)(2,1)}, u32[]{:S(2)}, u32[]{:S(2)}) collective-permute-start(bf16[256,4096]{1,0:T(8,128)(2,1)S(1)} %bitcast.46), channel_id=1, source_target_pairs={{0,32},{32,64},{64,96},{1,33},{33,65},{65,97},{2,34},{34,66},{66,9... | collective-permute-start | bytes 6291464 | tf_op jit(solution)/shard_map/while/body/eval_jaxpr/ppermute | solution.py:14
  564.2 29.1 %collective-permute-done = bf16[256,4096]{1,0:T(8,128)(2,1)} collective-permute-done((bf16[256,4096]{1,0:T(8,128)(2,1)S(1)}, bf16[256,4096]{1,0:T(8,128)(2,1)}, u32[]{:S(2)}, u32[]{:S(2)}) %collective-permute-start) | collective-permute-done | bytes 2097184 | tf_op jit(solution)/shard_map/while/body/eval_jaxpr/ppermute | solution.py:14
  593.3 40.7 %psum.7 = f32[8]{0:T(128)S(1)} all-reduce(f32[8]{0:T(128)S(1)} %broadcast_select_fusion), channel_id=1, replica_groups=mesh['segment'=4,'fsdp'=16,'rep'=2] {'segment'}, use_global_device_ids=true, to_apply=%region_14.15 | all-reduce | flops 8 | bytes 64 | tf_op jit(solution)/shard_map/psum | solution.py:19
  655.8 649.6 %reduce-scatter.3.cloned.1.call-done = f32[32,256]{1,0:T(8,128)} async-done(((f32[4096,256]{1,0:T(8,128)}), f32[32,256]{1,0:T(8,128)}) %reduce-scatter.3.cloned.1.call-update) | async-done | bytes 32784 | tf_op jit(solution)/shard_map/reduce_scatter | solution.py:186
  1305.3 648.7 %reduce-scatter.5.cloned.1.call-done = f32[32,256]{1,0:T(8,128)} async-done(((f32[4096,256]{1,0:T(8,128)}), f32[32,256]{1,0:T(8,128)}) %reduce-scatter.5.cloned.1.call-update) | async-done | bytes 32784 | tf_op jit(solution)/shard_map/reduce_scatter | solution.py:187
  (99 shorter events, 80.8 us)
Async XLA Ops:
  7.2 631.2 %all-gather.3.cloned.1.call-start = ((), (), s32[]{:S(2)}) async-start(), calls=%async_computation.3 | async-start | bytes 2228224 | tf_op jit(solution)/shard_map/all_gather | solution.py:139
  7.9 632.6 %all-gather.5.cloned.1.call-start = ((), (), s32[]{:S(2)}) async-start(), calls=%async_computation.4 | async-start | bytes 2228224 | tf_op jit(solution)/shard_map/all_gather | solution.py:140
  8.6 1296.7 %reduce-scatter.3.cloned.1.call-start = ((), (), s32[]{:S(2)}) async-start(), calls=%async_computation.5 | async-start | bytes 4227072 | tf_op jit(solution)/shard_map/reduce_scatter | solution.py:186
  12.5 4.3 copy-start.1
  12.5 4.3 copy-start.4
  16.8 576.4 %copy-start.3 = (f32[4096]{0:T(1024)S(1)}, f32[4096]{0:T(1024)}, u32[]{:S(2)}) copy-start(f32[4096]{0:T(1024)} %param.22) | copy-start | bytes 49156
  67.2 45.5 %collective-permute-start = (bf16[256,4096]{1,0:T(8,128)(2,1)S(1)}, bf16[256,4096]{1,0:T(8,128)(2,1)}, u32[]{:S(2)}, u32[]{:S(2)}) collective-permute-start(bf16[256,4096]{1,0:T(8,128)(2,1)S(1)} %bitcast.46), channel_id=1, source_target_pairs={{0,32},{32,64},{64,96},{1,33},{33,65},{65,97},{2,34},{34,66},{66,9... | collective-permute-start | bytes 6291464 | tf_op jit(solution)/shard_map/while/body/eval_jaxpr/ppermute | solution.py:14
  155.4 48.5 %collective-permute-start = (bf16[256,4096]{1,0:T(8,128)(2,1)S(1)}, bf16[256,4096]{1,0:T(8,128)(2,1)}, u32[]{:S(2)}, u32[]{:S(2)}) collective-permute-start(bf16[256,4096]{1,0:T(8,128)(2,1)S(1)} %bitcast.46), channel_id=1, source_target_pairs={{0,32},{32,64},{64,96},{1,33},{33,65},{65,97},{2,34},{34,66},{66,9... | collective-permute-start | bytes 6291464 | tf_op jit(solution)/shard_map/while/body/eval_jaxpr/ppermute | solution.py:14
  245.0 46.8 %collective-permute-start = (bf16[256,4096]{1,0:T(8,128)(2,1)S(1)}, bf16[256,4096]{1,0:T(8,128)(2,1)}, u32[]{:S(2)}, u32[]{:S(2)}) collective-permute-start(bf16[256,4096]{1,0:T(8,128)(2,1)S(1)} %bitcast.46), channel_id=1, source_target_pairs={{0,32},{32,64},{64,96},{1,33},{33,65},{65,97},{2,34},{34,66},{66,9... | collective-permute-start | bytes 6291464 | tf_op jit(solution)/shard_map/while/body/eval_jaxpr/ppermute | solution.py:14
  331.2 45.1 %collective-permute-start = (bf16[256,4096]{1,0:T(8,128)(2,1)S(1)}, bf16[256,4096]{1,0:T(8,128)(2,1)}, u32[]{:S(2)}, u32[]{:S(2)}) collective-permute-start(bf16[256,4096]{1,0:T(8,128)(2,1)S(1)} %bitcast.46), channel_id=1, source_target_pairs={{0,32},{32,64},{64,96},{1,33},{33,65},{65,97},{2,34},{34,66},{66,9... | collective-permute-start | bytes 6291464 | tf_op jit(solution)/shard_map/while/body/eval_jaxpr/ppermute | solution.py:14
  399.2 58.1 %collective-permute-start = (bf16[256,4096]{1,0:T(8,128)(2,1)S(1)}, bf16[256,4096]{1,0:T(8,128)(2,1)}, u32[]{:S(2)}, u32[]{:S(2)}) collective-permute-start(bf16[256,4096]{1,0:T(8,128)(2,1)S(1)} %bitcast.46), channel_id=1, source_target_pairs={{0,32},{32,64},{64,96},{1,33},{33,65},{65,97},{2,34},{34,66},{66,9... | collective-permute-start | bytes 6291464 | tf_op jit(solution)/shard_map/while/body/eval_jaxpr/ppermute | solution.py:14
  478.5 40.1 %collective-permute-start = (bf16[256,4096]{1,0:T(8,128)(2,1)S(1)}, bf16[256,4096]{1,0:T(8,128)(2,1)}, u32[]{:S(2)}, u32[]{:S(2)}) collective-permute-start(bf16[256,4096]{1,0:T(8,128)(2,1)S(1)} %bitcast.46), channel_id=1, source_target_pairs={{0,32},{32,64},{64,96},{1,33},{33,65},{65,97},{2,34},{34,66},{66,9... | collective-permute-start | bytes 6291464 | tf_op jit(solution)/shard_map/while/body/eval_jaxpr/ppermute | solution.py:14
  538.2 55.1 %collective-permute-start = (bf16[256,4096]{1,0:T(8,128)(2,1)S(1)}, bf16[256,4096]{1,0:T(8,128)(2,1)}, u32[]{:S(2)}, u32[]{:S(2)}) collective-permute-start(bf16[256,4096]{1,0:T(8,128)(2,1)S(1)} %bitcast.46), channel_id=1, source_target_pairs={{0,32},{32,64},{64,96},{1,33},{33,65},{65,97},{2,34},{34,66},{66,9... | collective-permute-start | bytes 6291464 | tf_op jit(solution)/shard_map/while/body/eval_jaxpr/ppermute | solution.py:14
  593.3 42.0 %copy-start.5 = (s32[8]{0:T(128)S(1)}, s32[8]{0:T(128)}, u32[]{:S(2)}) copy-start(s32[8]{0:T(128)} %param.18) | copy-start | bytes 100
  640.5 2.6 copy-start.2
  653.0 1301.0 %reduce-scatter.5.cloned.1.call-start = ((), (), s32[]{:S(2)}) async-start(), calls=%async_computation.6 | async-start | bytes 4227072 | tf_op jit(solution)/shard_map/reduce_scatter | solution.py:187
Sparse Core Ops, SparseCore 0:
  10.4 57.4 all-gather.2
  70.3 44.3 all-gather.4
  653.1 652.1 reduce-scatter.2
  1308.1 645.8 reduce-scatter.4
